TPU v7x, 32 devices: a whole 2x2x4 slice. The times are simulated.
32 devices in a mesh: seq: 16 (over z, x, core), head: 2 (over y).
Axes of the slice: x: 2, y: 2, z: 4, core: 2. Of those that a mesh axis runs over, the one named last changes fastest.
Arguments:
- step_tokens: bfloat16 [2, 12, 8, 2560], P(None, None, None, 'head'), may hold values from -6 to 6
- parents: int32 [2, 12, 8], replicated, may hold values from 0 to 7
- tail_cache: bfloat16 [12, 8, 64, 2048], P(None, 'head', 'seq'), may hold values from -192 to 192
- tail_len: int32 [12], replicated, may hold values from 0 to 62, as said below
- cache: bfloat16 [8, 2048, 2048], P(None, ('seq', 'head')), may hold values from -192 to 192
- cache_len: int32 [8], replicated, may hold values from 256 to 2048, as said below
- prompt_states: bfloat16 [4, 128, 2560], P(None, 'seq', 'head'), may hold values from -6 to 6
- prompt_len: int32 [4], replicated, may hold values from 32 to 128, as said below
- in_gain: float32 [2560], P('head'), may hold values from 0.5 to 1.5
- w_query: bfloat16 [2560, 2048], P('head', 'seq'), may hold values from -0.125 to 0.125
- w_keyval: bfloat16 [2560, 2048], P('head', 'seq'), may hold values from -0.125 to 0.125
- q_gain: float32 [256], replicated, may hold values from 0.6 to 32
- k_gain: float32 [256], replicated, may hold values from 0.6 to 32
- w_out: bfloat16 [2048, 2560], P('seq', 'head'), may hold values from -0.125 to 0.125
- post_gain: float32 [2560], P('head'), may hold values from 0.5 to 1.5
- ffn_gain: float32 [2560], P('head'), may hold values from 0.5 to 1.5
- w_gate: bfloat16 [2560, 10240], P('head', 'seq'), may hold values from -0.125 to 0.125
- w_up: bfloat16 [2560, 10240], P('head', 'seq'), may hold values from -0.125 to 0.125
- w_down: bfloat16 [10240, 2560], P('seq', 'head'), may hold values from -0.0625 to 0.0625
- final_gain: float32 [2560], P('head'), may hold values from 0.5 to 1.5
Outputs:
- decoded: bfloat16 [2, 12, 8, 2560], P(None, None, None, 'head')
Inputs may be any that keep to these rules, and one draw needn't show every extreme that they name: `tail_len`: the first 4 groups have 0; the largest entry is exactly 62. `cache_len`: the largest entry is exactly 2048. `prompt_len`: the largest entry is exactly 128.
All inputs are finite; a program needn't handle non-finite values.
Results may differ from a plain program's by a relative error of at most 0.0055.
The roundings to bfloat16 on the way count: a program that leaves them out, or rounds other values in their place, can miss the bound.
Values may be sent and summed in bfloat16 or wider, within the bound.
No kernel may reach another device: no remote copies, remote signals or barrier semaphores. Data moves between devices by JAX's collectives and lax.ppermute only.
A program may use at most 128 MiB of HBM per device.

v0:
```python
import jax
import jax.numpy as jnp
from jax import lax
from jax.sharding import PartitionSpec as P

D = 2560
QH = 8
KVH = 4
HD = 256
QD = 2048
EPS = 1e-06
NEG = -1e30
QSCALE = 0.0625


def norm_heads(values, gain, scale):
    shaped = values.reshape(values.shape[:-1] + (-1, gain.shape[0]))
    shaped = shaped * lax.rsqrt(jnp.mean(shaped * shaped, -1, keepdims=True) + EPS) * gain * scale
    return shaped.reshape(values.shape)


def finish_keys(pairs, k_gain):
    half = pairs.shape[-1] // 2
    keys = norm_heads(pairs[..., :half], k_gain, 1.0)
    return jnp.concatenate([keys, pairs[..., half:]], -1).astype(jnp.bfloat16)


def split_pairs(pairs):
    half = pairs.shape[-1] // 2
    keys = pairs[..., :half].reshape(pairs.shape[:-1] + (KVH, HD))
    values = pairs[..., half:].reshape(pairs.shape[:-1] + (KVH, HD))
    return (keys, values)


def project_tokens(tokens, in_gain, w_query, w_keyval, q_gain, k_gain):
    flat = tokens.reshape(-1, tokens.shape[-1]).astype(jnp.float32)
    scaled = (flat * in_gain).astype(jnp.bfloat16)
    q_part = jnp.dot(scaled, w_query, preferred_element_type=jnp.float32)
    kv_part = jnp.dot(scaled, w_keyval, preferred_element_type=jnp.float32)
    squares = jnp.sum(flat * flat, -1)
    q_part, kv_part, squares = lax.psum((q_part, kv_part, squares), "head")
    factor = lax.rsqrt(squares / D + EPS)[:, None]
    q_raw = (q_part * factor).astype(jnp.bfloat16)
    kv_raw = (kv_part * factor).astype(jnp.bfloat16)
    q_raw, kv_raw = (
        lax.all_gather(q_raw, "seq", axis=1, tiled=True),
        lax.all_gather(kv_raw, "seq", axis=1, tiled=True),
    )
    queries = norm_heads(q_raw.astype(jnp.float32), q_gain, QSCALE).astype(jnp.bfloat16)
    fresh = finish_keys(kv_raw.astype(jnp.float32), k_gain)
    return (queries, fresh)


def shards(
    step_tokens,
    parents,
    tail_cache,
    tail_len,
    cache,
    cache_len,
    prompt_states,
    prompt_len,
    in_gain,
    w_query,
    w_keyval,
    q_gain,
    k_gain,
    w_out,
    post_gain,
    ffn_gain,
    w_gate,
    w_up,
    w_down,
    final_gain,
):
    f32 = jnp.float32
    bf16 = jnp.bfloat16
    n_head = lax.axis_size("head")
    n_seq = lax.axis_size("seq")
    seq_at = lax.axis_index("seq")
    head_at = lax.axis_index("head")
    flat_at = seq_at * n_head + head_at
    steps, groups, beams, width = step_tokens.shape
    pre = prompt_states.shape[0]
    repeat = QH // KVH
    col_block = QD // n_seq
    block_head = jnp.arange(n_seq) * col_block // HD
    head_pick = (jnp.arange(QH)[:, None] == block_head[None, :]).astype(f32)
    rows = jnp.transpose(prompt_states, (1, 0, 2)).astype(f32)
    prompt_scaled = (rows * in_gain).astype(bf16).reshape(-1, width)
    prompt_squares = jnp.sum(rows * rows, -1).reshape(-1)
    prompt_terms = jnp.dot(
        prompt_scaled,
        lax.all_gather(w_keyval, "seq", axis=1, tiled=True),
        preferred_element_type=f32,
    )
    prompt_sum, prompt_sq = (
        lax.psum_scatter(prompt_terms, "head", scatter_dimension=0, tiled=True),
        lax.psum_scatter(prompt_squares, "head", scatter_dimension=0, tiled=True),
    )
    prompt_pairs = finish_keys(prompt_sum * lax.rsqrt(prompt_sq / D + EPS)[:, None], k_gain)
    prompt_seg = prompt_pairs.shape[0] // pre
    prompt_pairs = jnp.transpose(prompt_pairs.reshape(prompt_seg, pre, -1), (1, 0, 2))
    prompt_keys, prompt_values = split_pairs(prompt_pairs)
    prompt_ok = (flat_at * prompt_seg + jnp.arange(prompt_seg))[None, :] < prompt_len[:, None]
    cache_seg = cache.shape[1]
    cache_keys, cache_values = split_pairs(cache)
    cache_ok = (flat_at * cache_seg + jnp.arange(cache_seg))[None, :] < cache_len[:, None]
    tail_seg = tail_cache.shape[2]
    local_beams = tail_cache.shape[1]
    beam_ids = head_at * local_beams + jnp.arange(local_beams)
    offset = (seq_at * tail_seg + jnp.arange(tail_seg))[None, :] - tail_len[:, None]
    all_beams = jnp.arange(beams)
    every_query, every_fresh = project_tokens(
        step_tokens, in_gain, w_query, w_keyval, q_gain, k_gain
    )
    every_query = every_query.reshape(steps, groups, beams, -1)
    every_fresh = every_fresh.reshape(steps, groups, beams, -1)
    tail_state = tail_cache
    decoded = []
    for step in range(steps):
        query = every_query[step]
        new_pairs = every_fresh[step]
        everyone = lax.all_gather(tail_state, "head", axis=1, tiled=True)
        picks = lax.dynamic_slice_in_dim(parents[step], head_at * local_beams, local_beams, 1)
        tail_state = jnp.take_along_axis(everyone, picks[:, :, None, None], axis=1)
        owner = jnp.broadcast_to(all_beams[None, :, None], (groups, beams, tail_seg))
        mine = lax.dynamic_slice_in_dim(new_pairs, head_at * local_beams, local_beams, 1)
        tail_state = jnp.where((offset == step)[:, None, :, None], mine[:, :, None, :], tail_state)
        tail_ok = (offset <= step)[:, None, None, :] & (
            owner[:, :, None, :] == beam_ids[None, None, :, None]
        )
        shaped = query.reshape(groups, beams, KVH, repeat, HD)
        tail_keys, tail_values = split_pairs(tail_state)
        pre_scores = jnp.einsum(
            "gbkrd,gtkd->gbkrt", shaped[:pre], prompt_keys, preferred_element_type=f32
        )
        dec_scores = jnp.einsum(
            "gbkrd,gtkd->gbkrt", shaped[pre:], cache_keys, preferred_element_type=f32
        )
        tail_scores = jnp.einsum(
            "gbkrd,gctkd->gbkrct", shaped, tail_keys, preferred_element_type=f32
        )
        pre_mask = prompt_ok[:, None, None, None, :]
        dec_mask = cache_ok[:, None, None, None, :]
        tail_mask = tail_ok[:, :, None, None, :, :]
        pre_scores = jnp.where(pre_mask, pre_scores, NEG)
        dec_scores = jnp.where(dec_mask, dec_scores, NEG)
        tail_scores = jnp.where(tail_mask, tail_scores, NEG)
        top = jnp.concatenate([jnp.max(pre_scores, -1), jnp.max(dec_scores, -1)], 0)
        top = jnp.maximum(top, jnp.max(tail_scores, (-2, -1)))
        top = lax.pmax(top, ("seq", "head"))
        pre_weights = jnp.where(pre_mask, jnp.exp(pre_scores - top[:pre, ..., None]), 0.0)
        dec_weights = jnp.where(dec_mask, jnp.exp(dec_scores - top[pre:, ..., None]), 0.0)
        tail_weights = jnp.where(tail_mask, jnp.exp(tail_scores - top[..., None, None]), 0.0)
        total = jnp.concatenate([jnp.sum(pre_weights, -1), jnp.sum(dec_weights, -1)], 0)
        total = total + jnp.sum(tail_weights, (-2, -1))
        weighted = jnp.concatenate(
            [
                jnp.einsum(
                    "gbkrt,gtkd->gbkrd",
                    pre_weights.astype(bf16),
                    prompt_values,
                    preferred_element_type=f32,
                ),
                jnp.einsum(
                    "gbkrt,gtkd->gbkrd",
                    dec_weights.astype(bf16),
                    cache_values,
                    preferred_element_type=f32,
                ),
            ],
            0,
        )
        weighted = weighted + jnp.einsum(
            "gbkrct,gctkd->gbkrd",
            tail_weights.astype(bf16),
            tail_values,
            preferred_element_type=f32,
        )
        weighted = weighted.reshape(groups * beams, -1)
        total = total.reshape(groups * beams, -1)
        spread_total = jnp.sum(total[:, :, None] * head_pick[None, :, :], 1)
        share, own_total = (
            lax.psum_scatter(weighted, "seq", scatter_dimension=1, tiled=True),
            lax.psum_scatter(spread_total, "seq", scatter_dimension=1, tiled=True),
        )
        share, own_total = lax.psum((share, own_total), "head")
        attn = (share / own_total).astype(bf16)
        partial_out = jnp.dot(attn, w_out, preferred_element_type=f32)
        out_proj = lax.psum(partial_out, "seq")
        out_sq = lax.psum(jnp.sum(out_proj * out_proj, -1), "head")
        x_f = step_tokens[step].reshape(groups * beams, -1).astype(f32)
        state = (x_f + out_proj * lax.rsqrt(out_sq / D + EPS)[:, None] * post_gain).astype(bf16)
        state = lax.optimization_barrier(state)
        state_f = state.astype(f32)
        scaled_two = (state_f * ffn_gain).astype(bf16)
        gate_part = jnp.dot(scaled_two, w_gate, preferred_element_type=f32)
        up_part = jnp.dot(scaled_two, w_up, preferred_element_type=f32)
        gate_part, up_part, state_sq = lax.psum(
            (gate_part, up_part, jnp.sum(state_f * state_f, -1)), "head"
        )
        norm_s = lax.rsqrt(state_sq / D + EPS)[:, None]
        inner = (jax.nn.gelu(gate_part * norm_s, approximate=True) * (up_part * norm_s)).astype(
            bf16
        )
        ffn_out = lax.psum(jnp.dot(inner, w_down, preferred_element_type=f32), "seq")
        ffn_sq = lax.psum(jnp.sum(ffn_out * ffn_out, -1), "head")
        result = (state_f + ffn_out * lax.rsqrt(ffn_sq / D + EPS)[:, None] * final_gain).astype(
            bf16
        )
        decoded.append(result.reshape(groups, beams, -1))
    return jnp.stack(decoded)


def solution(mesh):
    return jax.shard_map(
        shards,
        mesh=mesh,
        in_specs=(
            P(None, None, None, "head"),
            P(),
            P(None, "head", "seq", None),
            P(),
            P(None, ("seq", "head"), None),
            P(),
            P(None, "seq", "head"),
            P(),
            P("head"),
            P("head", "seq"),
            P("head", "seq"),
            P(),
            P(),
            P("seq", "head"),
            P("head"),
            P("head"),
            P("head", "seq"),
            P("head", "seq"),
            P("seq", "head"),
            P("head"),
        ),
        out_specs=P(None, None, None, "head"),
        check_vma=False,
    )
```

profile of v0, /device:TPU:0, one launch (start us, length us, event | category | flops | bytes accessed | tf_op | source)
XLA Modules:
  0.0 628.8 jit_solution(9408125753058318404)
XLA Ops:
  7.9 1.9 fusion.145
  12.6 5.8 all-reduce.11
  19.1 17.0 %all-reduce.28.cloned.1.call-done = (f32[192,128]{1,0:T(8,128)}, f32[192,128]{1,0:T(8,128)}) async-done(((f32[192,128]{1,0:T(8,128)}, f32[192,128]{1,0:T(8,128)}), (f32[192,128]{1,0:T(8,128)}, f32[192,128]{1,0:T(8,128)})) %all-reduce.28.cloned.1.call-update) | async-done | bytes 196624 | tf_op jit(solution)/shard_map/psum | solution.py:41
  37.1 23.5 %all_gather.17 = bf16[192,2048]{1,0:T(8,128)(2,1)S(1)} all-gather(bf16[192,128]{1,0:T(8,128)(2,1)S(1)} %get-tuple-element.70), channel_id=1, replica_groups=mesh['seq'=16,'head'=2] {'seq'}, dimensions={1}, use_global_device_ids=true | all-gather | bytes 835584 | tf_op jit(solution)/shard_map/all_gather | solution.py:47
  66.4 2.9 gather_fusion
  73.5 2.7 fusion.131
  77.9 1.9 reshape.375
  83.1 22.2 %all_gather.16 = bf16[192,2048]{1,0:T(8,128)(2,1)S(1)} all-gather(bf16[192,128]{1,0:T(8,128)(2,1)S(1)} %get-tuple-element.71), channel_id=1, replica_groups=mesh['seq'=16,'head'=2] {'seq'}, dimensions={1}, use_global_device_ids=true | all-gather | bytes 835584 | tf_op jit(solution)/shard_map/all_gather | solution.py:46
  105.5 1.8 copy.246
  107.2 2.4 reduce_sum.180
  121.2 2.0 fusion.37
  124.3 4.0 gather_fusion.1
  128.3 1.9 select_select_fusion
  130.2 28.0 %all-gather.4.cloned.1.call-done = bf16[1280,2048]{1,0:T(8,128)(2,1)} async-done(((bf16[1280,128]{1,0:T(8,128)(2,1)}), bf16[1280,2048]{1,0:T(8,128)(2,1)}) %all-gather.4.cloned.1.call-update) | async-done | bytes 5242896 | tf_op jit(solution)/shard_map/all_gather | solution.py:94
  158.2 4.2 fusion.143
  164.5 2.1 fusion.34
  167.7 4.7 reduce-scatter.4.cloned.1.call-done
  173.9 1.9 fusion.142
  175.9 1.9 fusion.140
  177.9 40.8 %all-reduce.3 = (f32[12,8,4,2]{1,3,2,0:T(2,128)S(1)}, f32[12,8,4,2]{1,3,2,0:T(2,128)S(1)}) all-reduce(f32[12,8,4,2]{1,3,2,0:T(2,128)S(1)} %maximum_maximum_fusion.1, f32[12,8,4,2]{1,3,2,0:T(2,128)S(1)} %maximum_maximum_fusion), channel_id=1, replica_groups=mesh['seq'=16,'head'=2] {'seq','head'}, use_global_device_ids=true, to_apply=%region_35.37 | all-reduce | flops 1536 | bytes 12288 | tf_op jit(solution)/shard_map/pmax | solution.py:152
  235.1 60.1 %all-reduce.4 = (f32[96,16]{0,1:T(8,128)S(1)}, f32[96,16]{0,1:T(8,128)S(1)}) all-reduce(f32[96,16]{0,1:T(8,128)S(1)} %get-tuple-element.7, f32[96,16]{0,1:T(8,128)S(1)} %get-tuple-element.6), channel_id=7, replica_groups=mesh['seq'=16,'head'=2] {'seq'}, use_global_device_ids=true, to_apply=%region_42.44.clone | all-reduce | flops 3072 | bytes 24576
  297.6 45.9 %reduce-scatter.8.cloned.1.call-done = f32[96,128]{1,0:T(8,128)} async-done(((f32[96,2048]{1,0:T(8,128)}), f32[96,128]{1,0:T(8,128)}) %reduce-scatter.8.cloned.1.call-update) | async-done | bytes 49168 | tf_op jit(solution)/shard_map/reduce_scatter | solution.py:185
  343.6 22.5 %all-reduce.24.cloned.1.call-done = (f32[96,128]{1,0:T(8,128)}, f32[96]{0:T(128)}, f32[96,128]{1,0:T(8,128)}, f32[96]{0:T(128)}) async-done(((f32[96,128]{1,0:T(8,128)}, f32[96]{0:T(128)}, f32[96,128]{1,0:T(8,128)}, f32[96]{0:T(128)}), (f32[96,128]{1,0:T(8,128)}, f32[96]{0:T(128)}, f32[96,128]{1,0:T(8,128)}, f32[96]{0:T(128)})) %all-reduce.24.cloned.1.call-update) | async-done | bytes 99088 | tf_op jit(solution)/shard_map/psum | solution.py:188
  366.1 1.9 fusion.111
  367.9 1.9 fusion.110
  369.9 94.0 %all-reduce.22.cloned.1.call-done = (f32[96,1280]{1,0:T(8,128)}, f32[96,1280]{1,0:T(8,128)}) async-done(((f32[96,1280]{1,0:T(8,128)}, f32[96,1280]{1,0:T(8,128)}), (f32[96,1280]{1,0:T(8,128)}, f32[96,1280]{1,0:T(8,128)})) %all-reduce.22.cloned.1.call-update) | async-done | bytes 983056 | tf_op jit(solution)/shard_map/psum | solution.py:191
  466.2 4.9 all-reduce.9
  477.7 4.9 all-reduce.8
  482.7 33.1 %all-reduce.26.cloned.1.call-done = (f32[96,640]{1,0:T(8,128)}, f32[96,640]{1,0:T(8,128)}, f32[96,640]{1,0:T(8,128)}, f32[96,640]{1,0:T(8,128)}) async-done(((f32[96,640]{1,0:T(8,128)}, f32[96,640]{1,0:T(8,128)}, f32[96,640]{1,0:T(8,128)}, f32[96,640]{1,0:T(8,128)}), (f32[96,640]{1,0:T(8,128)}, f32[96,640]{1,0:T(8,128)}, f32[96,640]{1,0:T(8,128)}, f32[96,640]{1,0:T(8,128)})) %all-reduce.26.cloned.1.call-update) | async-done | bytes 983056 | tf_op jit(solution)/shard_map/psum | solution.py:200
  515.7 2.4 fusion.81
  519.5 93.3 %all-reduce.20.cloned.1.call-done = (f32[96,1280]{1,0:T(8,128)}, f32[96,1280]{1,0:T(8,128)}) async-done(((f32[96,1280]{1,0:T(8,128)}, f32[96,1280]{1,0:T(8,128)}), (f32[96,1280]{1,0:T(8,128)}, f32[96,1280]{1,0:T(8,128)})) %all-reduce.20.cloned.1.call-update) | async-done | bytes 983056 | tf_op jit(solution)/shard_map/psum | solution.py:207
  615.1 4.9 all-reduce.7
  (274 shorter events, 70.4 us)
Async XLA Ops:
  6.5 509.2 %copy-start = (bf16[640,1280]{1,0:T(8,128)(2,1)S(1)}, bf16[640,1280]{1,0:T(8,128)(2,1)}, u32[]{:S(2)}) copy-start(bf16[640,1280]{1,0:T(8,128)(2,1)} %param.40) | copy-start | bytes 4915204
  6.5 29.6 %all-reduce.28.cloned.1.call-start = ((), (), s32[]{:S(2)}) async-start(), calls=%async_computation.13 | async-start | bytes 393216 | tf_op jit(solution)/shard_map/psum | solution.py:41
  7.9 10.6 %copy-start.47 = (s32[12]{0:T(128)S(1)}, s32[12]{0:T(128)}, u32[]{:S(2)}) copy-start(s32[12]{0:T(128)} %param.25) | copy-start | bytes 148
  10.8 55.7 %all-gather.6.cloned.1.call-start = ((), (), s32[]{:S(2)}) async-start(), calls=%async_computation.5 | async-start | bytes 2359296 | tf_op jit(solution)/shard_map/all_gather | solution.py:124
  11.5 112.7 %all-gather.8.cloned.1.call-start = ((), (), s32[]{:S(2)}) async-start(), calls=%async_computation.7 | async-start | bytes 2359296 | tf_op jit(solution)/shard_map/all_gather | solution.py:124
  11.8 52.8 %copy-start.32 = (f32[1,2,4,128]{3,1,2,0:T(2,128)}, f32[1,2,4,128]{3,1,2,0:T(2,128)S(1)}, u32[]{:S(2)}) copy-start(f32[1,2,4,128]{3,1,2,0:T(2,128)S(1)} %copy.245) | copy-start | bytes 12292
  71.1 87.1 %all-gather.4.cloned.1.call-start = ((), (), s32[]{:S(2)}) async-start(), calls=%async_computation.3 | async-start | bytes 5570560 | tf_op jit(solution)/shard_map/all_gather | solution.py:94
  71.6 100.7 %reduce-scatter.4.cloned.1.call-start = ((), (), s32[]{:S(2)}) async-start(), calls=%async_computation.4 | async-start | bytes 393216 | tf_op jit(solution)/shard_map/reduce_scatter | solution.py:98
  76.3 5.4 copy-start.50
  76.3 6.1 copy-start.49
  82.4 33.9 %copy-start.35 = (pred[8,64]{1,0:T(8,128)(4,1)}, pred[8,64]{1,0:T(8,128)(4,1)S(1)}, u32[]{:S(2)}) copy-start(pred[8,64]{1,0:T(8,128)(4,1)S(1)} %broadcast_compare_fusion) | copy-start | bytes 1540
  83.1 41.0 %copy-start.24 = (pred[12,8,4,4]{0,1,3,2:T(8,128)(4,1)}, pred[12,8,4,4]{0,1,3,2:T(8,128)(4,1)S(1)}, u32[]{:S(2)}) copy-start(pred[12,8,4,4]{0,1,3,2:T(8,128)(4,1)S(1)} %get-tuple-element.72) | copy-start | bytes 4612
  123.2 5.0 copy-start.15
  123.2 5.0 copy-start.39
  124.3 33.9 %copy-start.17 = (bf16[32,1280]{1,0:T(8,128)(2,1)S(1)}, bf16[32,1280]{1,0:T(8,128)(2,1)}, u32[]{:S(2)}) copy-start(bf16[32,1280]{1,0:T(8,128)(2,1)} %reshape.371) | copy-start | bytes 245764
  162.4 135.2 %reduce-scatter.6.cloned.1.call-start = ((), (), s32[]{:S(2)}) async-start(), calls=%async_computation.6 | async-start | bytes 835584 | tf_op jit(solution)/shard_map/reduce_scatter | solution.py:185
  164.5 7.9 %copy-start.46 = (f32[16]{0:T(128)S(1)}, f32[16]{0:T(128)}, u32[]{:S(2)}) copy-start(f32[16]{0:T(128)} %fusion.118) | copy-start | bytes 196
  166.6 7.1 %copy-start.33 = (f32[1,2,4,128]{3,1,2,0:T(2,128)S(1)}, f32[1,2,4,128]{3,1,2,0:T(2,128)}, u32[]{:S(2)}) copy-start(f32[1,2,4,128]{3,1,2,0:T(2,128)} %copy-done.32) | copy-start | bytes 12292
  167.5 6.4 %copy-start.42 = (pred[4,4]{1,0:T(4,128)(4,1)S(1)}, pred[4,4]{1,0:T(4,128)(4,1)}, u32[]{:S(2)}) copy-start(pred[4,4]{1,0:T(4,128)(4,1)} %broadcast_compare_fusion.1) | copy-start | bytes 52
  167.5 10.3 %copy-start.29 = (f32[8,8,4,2]{1,3,2,0:T(2,128)S(1)}, f32[8,8,4,2]{1,3,2,0:T(2,128)}, u32[]{:S(2)}) copy-start(f32[8,8,4,2]{1,3,2,0:T(2,128)} %get-tuple-element.78) | copy-start | bytes 6148
  167.5 10.4 %copy-start.28 = (f32[8,8,4,2]{1,3,2,0:T(2,128)S(1)}, f32[8,8,4,2]{1,3,2,0:T(2,128)}, u32[]{:S(2)}) copy-start(f32[8,8,4,2]{1,3,2,0:T(2,128)} %get-tuple-element.74) | copy-start | bytes 6148
  173.8 50.0 %copy-start.12 = (f32[8,8,4,2,64]{4,1,3,2,0:T(8,128)S(1)}, f32[8,8,4,2,64]{4,1,3,2,0:T(8,128)}, u32[]{:S(2)}) copy-start(f32[8,8,4,2,64]{4,1,3,2,0:T(8,128)} %get-tuple-element.79) | copy-start | bytes 393220
  226.8 116.6 %reduce-scatter.8.cloned.1.call-start = ((), (), s32[]{:S(2)}) async-start(), calls=%async_computation.8 | async-start | bytes 835584 | tf_op jit(solution)/shard_map/reduce_scatter | solution.py:185
  233.1 133.0 %copy-start.10 = (bf16[128,1280]{1,0:T(8,128)(2,1)S(1)}, bf16[128,1280]{1,0:T(8,128)(2,1)}, u32[]{:S(2)}) copy-start(bf16[128,1280]{1,0:T(8,128)(2,1)} %param.35) | copy-start | bytes 983044
  233.1 133.0 %all-reduce.24.cloned.1.call-start = ((), (), s32[]{:S(2)}) async-start(), calls=%async_computation.11 | async-start | bytes 198656 | tf_op jit(solution)/shard_map/psum | solution.py:188
  343.5 120.4 %all-reduce.22.cloned.1.call-start = ((), (), s32[]{:S(2)}) async-start(), calls=%async_computation.10 | async-start | bytes 1966080 | tf_op jit(solution)/shard_map/psum | solution.py:191
  367.9 103.3 %copy-start.37 = (f32[1280]{0:T(1024)S(1)}, f32[1280]{0:T(1024)}, u32[]{:S(2)}) copy-start(f32[1280]{0:T(1024)} %param.36) | copy-start | bytes 15364
  369.8 103.1 %copy-start.2 = (bf16[1280,640]{1,0:T(8,128)(2,1)S(1)}, bf16[1280,640]{1,0:T(8,128)(2,1)}, u32[]{:S(2)}) copy-start(bf16[1280,640]{1,0:T(8,128)(2,1)} %param.39) | copy-start | bytes 4915204
  369.8 103.1 %copy-start.26 = (f32[1280]{0:T(1024)S(1)}, f32[1280]{0:T(1024)}, u32[]{:S(2)}) copy-start(f32[1280]{0:T(1024)} %param.37) | copy-start | bytes 15364
  369.9 145.9 %all-reduce.26.cloned.1.call-start = ((), (), s32[]{:S(2)}) async-start(), calls=%async_computation.12 | async-start | bytes 1966080 | tf_op jit(solution)/shard_map/psum | solution.py:200
  477.4 135.4 %all-reduce.20.cloned.1.call-start = ((), (), s32[]{:S(2)}) async-start(), calls=%async_computation.9 | async-start | bytes 1966080 | tf_op jit(solution)/shard_map/psum | solution.py:207
  519.4 100.6 %copy-start.38 = (f32[1280]{0:T(1024)S(1)}, f32[1280]{0:T(1024)}, u32[]{:S(2)}) copy-start(f32[1280]{0:T(1024)} %param.41) | copy-start | bytes 15364
  (32 other events, 88.4 us)
Sparse Core Ops, SparseCore 0:
  10.9 25.1 all-reduce.27
  37.6 27.1 all-gather.5
  71.2 25.6 all-gather.7
  98.9 59.2 all-gather.3
  162.5 9.8 reduce-scatter.3
  227.0 57.3 reduce-scatter.5
  287.9 55.5 reduce-scatter.7
  346.1 19.9 all-reduce.23
  370.0 93.8 all-reduce.21
  477.5 38.1 all-reduce.25
  519.6 93.1 all-reduce.19
where the time goes:
time: 630 us; the launch traced here: 629 us
  waiting for transfers between devices  340 us (54%)
  blocking collectives  167 us (27%)
  local copies, waits for them, and re-layouts  40.9 us (6%)
  matrix products  38.3 us (6%)
  other arithmetic  27.2 us (4%)
  between operations  14.9 us (2%)
    psum x1, waiting for transfers between devices, shards(): out_proj = lax.psum(partial_out, 'seq')  94 us
    psum x1, waiting for transfers between devices, shards(): lax.psum(jnp.dot(inner, w_down, preferred_element_type=f32), 'seq')  93.3 us
    unnamed x1, blocking collectives  60.1 us
    reduce_scatter x2, waiting for transfers between devices, shards(): lax.psum_scatter(weighted, 'seq', scatter_dimension=1, tiled=True)  45.9 us
    pmax x1, blocking collectives, shards(): top = lax.pmax(top, ('seq', 'head'))  40.8 us
    psum x1, waiting for transfers between devices, shards(): lax.psum((gate_part, up_part, jnp.sum(state_f * state_f, -1)), 'head')  33.1 us
    all_gather x1, waiting for transfers between devices, shards(): lax.all_gather(w_keyval, 'seq', axis=1, tiled=True)  28 us
    all_gather x1, blocking collectives, project_tokens(): lax.all_gather(kv_raw, 'seq', axis=1, tiled=True)  23.5 us
  transfers between devices with their start and end apart: 11, of which 8 were waited for; matrix products, arithmetic and copies ran while one was open for 9% of the time, Pallas kernels for 0%

commit v1 on v0

--- a/solution.py
+++ b/solution.py
@@ -204,7 +204,9 @@
         inner = (jax.nn.gelu(gate_part * norm_s, approximate=True) * (up_part * norm_s)).astype(
             bf16
         )
-        ffn_out = lax.psum(jnp.dot(inner, w_down, preferred_element_type=f32), "seq")
+        s0 = jnp.dot(inner, w_down, preferred_element_type=f32)
+        w1 = jax.lax.all_gather(s0, "seq")
+        ffn_out = jnp.sum(w1, axis=0)
         ffn_sq = lax.psum(jnp.sum(ffn_out * ffn_out, -1), "head")
         result = (state_f + ffn_out * lax.rsqrt(ffn_sq / D + EPS)[:, None] * final_gain).astype(
             bf16

time: 630 us -> 681 us (1.081)
  waiting for transfers between devices: 340 us -> 383 us
    all_gather x0 -> x2, waiting for transfers between devices: none -> 139 us  [shards(): w1 = jax.lax.all_gather(s0, 'seq')]
    psum x1 -> x0, waiting for transfers between devices: 93.3 us -> none  [shards(): lax.psum(jnp.dot(inner, w_down, preferred_element_type=f32), 'seq')]
    reduce_sum x0 -> x2, other arithmetic: none -> 7.33 us  [shards(): ffn_out = jnp.sum(w1, axis=0)]
  transfers between devices with their start and end apart: 11 -> 12, of which waited for: 8 -> 9; matrix products, arithmetic and copies ran while one was open for 9% -> 10% of each run, Pallas kernels for 0% -> 0%
where the time goes in v1:
time: 681 us; the launch traced here: 679 us
  waiting for transfers between devices  383 us (56%)
  blocking collectives  167 us (25%)
  local copies, waits for them, and re-layouts  44.6 us (7%)
  matrix products  37.1 us (5%)
  other arithmetic  32.2 us (5%)
  between operations  15.2 us (2%)
    all_gather x2, waiting for transfers between devices, shards(): w1 = jax.lax.all_gather(s0, 'seq')  139 us
    psum x1, waiting for transfers between devices, shards(): out_proj = lax.psum(partial_out, 'seq')  94 us
    unnamed x1, blocking collectives  60 us
    reduce_scatter x2, waiting for transfers between devices, shards(): lax.psum_scatter(weighted, 'seq', scatter_dimension=1, tiled=True)  46.2 us
    pmax x1, blocking collectives, shards(): top = lax.pmax(top, ('seq', 'head'))  40.8 us
    psum x1, waiting for transfers between devices, shards(): lax.psum((gate_part, up_part, jnp.sum(state_f * state_f, -1)), 'head')  33.1 us
    all_gather x1, waiting for transfers between devices, shards(): lax.all_gather(w_keyval, 'seq', axis=1, tiled=True)  27.8 us
    all_gather x1, blocking collectives, project_tokens(): lax.all_gather(kv_raw, 'seq', axis=1, tiled=True)  23.5 us
  transfers between devices with their start and end apart: 12, of which 9 were waited for; matrix products, arithmetic and copies ran while one was open for 10% of the time, Pallas kernels for 0%

profile of v1, /device:TPU:0, one launch (start us, length us, event | category | flops | bytes accessed | tf_op | source)
XLA Modules:
  0.0 679.4 jit_solution(2569992698711636921)
XLA Ops:
  7.9 1.9 fusion.145
  12.6 5.8 all-reduce.10
  19.1 17.0 %all-reduce.24.cloned.1.call-done = (f32[192,128]{1,0:T(8,128)}, f32[192,128]{1,0:T(8,128)}) async-done(((f32[192,128]{1,0:T(8,128)}, f32[192,128]{1,0:T(8,128)}), (f32[192,128]{1,0:T(8,128)}, f32[192,128]{1,0:T(8,128)})) %all-reduce.24.cloned.1.call-update) | async-done | bytes 196624 | tf_op jit(solution)/shard_map/psum | solution.py:41
  37.1 23.5 %all_gather.29 = bf16[192,2048]{1,0:T(8,128)(2,1)S(1)} all-gather(bf16[192,128]{1,0:T(8,128)(2,1)S(1)} %get-tuple-element.68), channel_id=1, replica_groups=mesh['seq'=16,'head'=2] {'seq'}, dimensions={1}, use_global_device_ids=true | all-gather | bytes 835584 | tf_op jit(solution)/shard_map/all_gather | solution.py:47
  66.5 2.9 gather_fusion
  73.4 2.7 fusion.131
  77.9 1.9 reshape.375
  83.2 22.2 %all_gather.28 = bf16[192,2048]{1,0:T(8,128)(2,1)S(1)} all-gather(bf16[192,128]{1,0:T(8,128)(2,1)S(1)} %get-tuple-element.69), channel_id=1, replica_groups=mesh['seq'=16,'head'=2] {'seq'}, dimensions={1}, use_global_device_ids=true | all-gather | bytes 835584 | tf_op jit(solution)/shard_map/all_gather | solution.py:46
  107.3 2.4 reduce_sum.198
  121.3 2.1 fusion.37
  124.5 3.9 gather_fusion.1
  128.4 1.9 select_select_fusion
  130.3 27.8 %all-gather.8.cloned.1.call-done = bf16[1280,2048]{1,0:T(8,128)(2,1)} async-done(((bf16[1280,128]{1,0:T(8,128)(2,1)}), bf16[1280,2048]{1,0:T(8,128)(2,1)}) %all-gather.8.cloned.1.call-update) | async-done | bytes 5242896 | tf_op jit(solution)/shard_map/all_gather | solution.py:94
  158.1 4.2 fusion.143
  164.8 2.9 fusion.34
  167.7 2.0 copy.201
  170.5 1.9 reduce-scatter.4.cloned.1.call-done
  178.1 40.8 %all-reduce.3 = (f32[12,8,4,2]{1,3,2,0:T(2,128)S(1)}, f32[12,8,4,2]{1,3,2,0:T(2,128)S(1)}) all-reduce(f32[12,8,4,2]{1,3,2,0:T(2,128)S(1)} %maximum_maximum_fusion.1, f32[12,8,4,2]{1,3,2,0:T(2,128)S(1)} %maximum_maximum_fusion), channel_id=1, replica_groups=mesh['seq'=16,'head'=2] {'seq','head'}, use_global_device_ids=true, to_apply=%region_35.37 | all-reduce | flops 1536 | bytes 12288 | tf_op jit(solution)/shard_map/pmax | solution.py:152
  235.6 60.0 %all-reduce.4 = (f32[96,16]{0,1:T(8,128)S(1)}, f32[96,16]{0,1:T(8,128)S(1)}) all-reduce(f32[96,16]{0,1:T(8,128)S(1)} %get-tuple-element.7, f32[96,16]{0,1:T(8,128)S(1)} %get-tuple-element.6), channel_id=9, replica_groups=mesh['seq'=16,'head'=2] {'seq'}, use_global_device_ids=true, to_apply=%region_42.44.clone | all-reduce | flops 3072 | bytes 24576
  298.0 46.2 %reduce-scatter.8.cloned.1.call-done = f32[96,128]{1,0:T(8,128)} async-done(((f32[96,2048]{1,0:T(8,128)}), f32[96,128]{1,0:T(8,128)}) %reduce-scatter.8.cloned.1.call-update) | async-done | bytes 49168 | tf_op jit(solution)/shard_map/reduce_scatter | solution.py:185
  344.3 22.5 %all-reduce.20.cloned.1.call-done = (f32[96,128]{1,0:T(8,128)}, f32[96]{0:T(128)}, f32[96,128]{1,0:T(8,128)}, f32[96]{0:T(128)}) async-done(((f32[96,128]{1,0:T(8,128)}, f32[96]{0:T(128)}, f32[96,128]{1,0:T(8,128)}, f32[96]{0:T(128)}), (f32[96,128]{1,0:T(8,128)}, f32[96]{0:T(128)}, f32[96,128]{1,0:T(8,128)}, f32[96]{0:T(128)})) %all-reduce.20.cloned.1.call-update) | async-done | bytes 99088 | tf_op jit(solution)/shard_map/psum | solution.py:188
  368.6 1.9 fusion.110
  370.6 94.0 %all-reduce.18.cloned.1.call-done = (f32[96,1280]{1,0:T(8,128)}, f32[96,1280]{1,0:T(8,128)}) async-done(((f32[96,1280]{1,0:T(8,128)}, f32[96,1280]{1,0:T(8,128)}), (f32[96,1280]{1,0:T(8,128)}, f32[96,1280]{1,0:T(8,128)})) %all-reduce.18.cloned.1.call-update) | async-done | bytes 983056 | tf_op jit(solution)/shard_map/psum | solution.py:191
  466.9 4.9 all-reduce.8
  478.4 4.9 all-reduce.7
  483.3 33.1 %all-reduce.22.cloned.1.call-done = (f32[96,640]{1,0:T(8,128)}, f32[96,640]{1,0:T(8,128)}, f32[96,640]{1,0:T(8,128)}, f32[96,640]{1,0:T(8,128)}) async-done(((f32[96,640]{1,0:T(8,128)}, f32[96,640]{1,0:T(8,128)}, f32[96,640]{1,0:T(8,128)}, f32[96,640]{1,0:T(8,128)}), (f32[96,640]{1,0:T(8,128)}, f32[96,640]{1,0:T(8,128)}, f32[96,640]{1,0:T(8,128)}, f32[96,640]{1,0:T(8,128)})) %all-reduce.22.cloned.1.call-update) | async-done | bytes 983056 | tf_op jit(solution)/shard_map/psum | solution.py:200
  516.4 2.4 fusion.83
  520.2 70.3 %all-gather.14.cloned.1.call-done = f32[1536,1280]{1,0:T(8,128)} async-done(((f32[96,1280]{1,0:T(8,128)}), f32[1536,1280]{1,0:T(8,128)}) %all-gather.14.cloned.1.call-update) | async-done | bytes 7864336 | tf_op jit(solution)/shard_map/all_gather | solution.py:208
  590.5 3.7 reduce_sum.206
  594.2 68.4 %all-gather.16.cloned.1.call-done = f32[1536,1280]{1,0:T(8,128)} async-done(((f32[96,1280]{1,0:T(8,128)}), f32[1536,1280]{1,0:T(8,128)}) %all-gather.16.cloned.1.call-update) | async-done | bytes 7864336 | tf_op jit(solution)/shard_map/all_gather | solution.py:208
  662.6 3.7 reduce_sum.214
  666.5 4.9 all-reduce.6
  (261 shorter events, 75.5 us)
Async XLA Ops:
  6.5 509.8 %copy-start = (bf16[640,1280]{1,0:T(8,128)(2,1)S(1)}, bf16[640,1280]{1,0:T(8,128)(2,1)}, u32[]{:S(2)}) copy-start(bf16[640,1280]{1,0:T(8,128)(2,1)} %param.40) | copy-start | bytes 4915204
  6.5 29.6 %all-reduce.24.cloned.1.call-start = ((), (), s32[]{:S(2)}) async-start(), calls=%async_computation.14 | async-start | bytes 393216 | tf_op jit(solution)/shard_map/psum | solution.py:41
  7.9 4.4 copy-start.23
  7.9 10.6 %copy-start.39 = (s32[12]{0:T(128)S(1)}, s32[12]{0:T(128)}, u32[]{:S(2)}) copy-start(s32[12]{0:T(128)} %param.25) | copy-start | bytes 148
  10.8 55.7 %all-gather.10.cloned.1.call-start = ((), (), s32[]{:S(2)}) async-start(), calls=%async_computation.5 | async-start | bytes 2359296 | tf_op jit(solution)/shard_map/all_gather | solution.py:124
  11.5 113.0 %all-gather.12.cloned.1.call-start = ((), (), s32[]{:S(2)}) async-start(), calls=%async_computation.7 | async-start | bytes 2359296 | tf_op jit(solution)/shard_map/all_gather | solution.py:124
  11.8 52.8 %copy-start.24 = (f32[1,2,4,128]{3,1,2,0:T(2,128)}, f32[1,2,4,128]{3,1,2,0:T(2,128)S(1)}, u32[]{:S(2)}) copy-start(f32[1,2,4,128]{3,1,2,0:T(2,128)S(1)} %copy.245) | copy-start | bytes 12292
  71.0 87.1 %all-gather.8.cloned.1.call-start = ((), (), s32[]{:S(2)}) async-start(), calls=%async_computation.3 | async-start | bytes 5570560 | tf_op jit(solution)/shard_map/all_gather | solution.py:94
  71.6 100.7 %reduce-scatter.4.cloned.1.call-start = ((), (), s32[]{:S(2)}) async-start(), calls=%async_computation.4 | async-start | bytes 393216 | tf_op jit(solution)/shard_map/reduce_scatter | solution.py:98
  76.2 5.6 copy-start.41
  76.2 6.2 copy-start.40
  82.5 33.9 %copy-start.27 = (pred[8,64]{1,0:T(8,128)(4,1)}, pred[8,64]{1,0:T(8,128)(4,1)S(1)}, u32[]{:S(2)}) copy-start(pred[8,64]{1,0:T(8,128)(4,1)S(1)} %broadcast_compare_fusion) | copy-start | bytes 1540
  83.2 41.1 %copy-start.18 = (pred[12,8,4,4]{0,1,3,2:T(8,128)(4,1)}, pred[12,8,4,4]{0,1,3,2:T(8,128)(4,1)S(1)}, u32[]{:S(2)}) copy-start(pred[12,8,4,4]{0,1,3,2:T(8,128)(4,1)S(1)} %get-tuple-element.70) | copy-start | bytes 4612
  123.4 5.0 copy-start.31
  123.4 5.0 copy-start.32
  124.5 33.6 %copy-start.13 = (bf16[32,1280]{1,0:T(8,128)(2,1)S(1)}, bf16[32,1280]{1,0:T(8,128)(2,1)}, u32[]{:S(2)}) copy-start(bf16[32,1280]{1,0:T(8,128)(2,1)} %reshape.371) | copy-start | bytes 245764
  162.3 135.7 %reduce-scatter.6.cloned.1.call-start = ((), (), s32[]{:S(2)}) async-start(), calls=%async_computation.6 | async-start | bytes 835584 | tf_op jit(solution)/shard_map/reduce_scatter | solution.py:185
  164.8 4.8 copy-start.16
  164.8 7.5 %copy-start.38 = (f32[16]{0:T(128)S(1)}, f32[16]{0:T(128)}, u32[]{:S(2)}) copy-start(f32[16]{0:T(128)} %fusion.118) | copy-start | bytes 196
  167.7 5.9 copy-start.25
  167.7 6.1 copy-start.34
  227.6 116.6 %reduce-scatter.8.cloned.1.call-start = ((), (), s32[]{:S(2)}) async-start(), calls=%async_computation.8 | async-start | bytes 835584 | tf_op jit(solution)/shard_map/reduce_scatter | solution.py:185
  233.5 133.2 %copy-start.8 = (bf16[128,1280]{1,0:T(8,128)(2,1)S(1)}, bf16[128,1280]{1,0:T(8,128)(2,1)}, u32[]{:S(2)}) copy-start(bf16[128,1280]{1,0:T(8,128)(2,1)} %param.35) | copy-start | bytes 983044
  233.6 133.2 %all-reduce.20.cloned.1.call-start = ((), (), s32[]{:S(2)}) async-start(), calls=%async_computation.12 | async-start | bytes 198656 | tf_op jit(solution)/shard_map/psum | solution.py:188
  344.2 120.3 %all-reduce.18.cloned.1.call-start = ((), (), s32[]{:S(2)}) async-start(), calls=%async_computation.11 | async-start | bytes 1966080 | tf_op jit(solution)/shard_map/psum | solution.py:191
  368.6 103.3 %copy-start.29 = (f32[1280]{0:T(1024)S(1)}, f32[1280]{0:T(1024)}, u32[]{:S(2)}) copy-start(f32[1280]{0:T(1024)} %param.36) | copy-start | bytes 15364
  370.5 103.1 %copy-start.2 = (bf16[1280,640]{1,0:T(8,128)(2,1)S(1)}, bf16[1280,640]{1,0:T(8,128)(2,1)}, u32[]{:S(2)}) copy-start(bf16[1280,640]{1,0:T(8,128)(2,1)} %param.39) | copy-start | bytes 4915204
  370.5 103.1 %copy-start.20 = (f32[1280]{0:T(1024)S(1)}, f32[1280]{0:T(1024)}, u32[]{:S(2)}) copy-start(f32[1280]{0:T(1024)} %param.37) | copy-start | bytes 15364
  370.5 145.9 %all-reduce.22.cloned.1.call-start = ((), (), s32[]{:S(2)}) async-start(), calls=%async_computation.13 | async-start | bytes 1966080 | tf_op jit(solution)/shard_map/psum | solution.py:200
  478.0 112.5 %all-gather.14.cloned.1.call-start = ((), (), s32[]{:S(2)}) async-start(), calls=%async_computation.9 | async-start | bytes 8355840 | tf_op jit(solution)/shard_map/all_gather | solution.py:208
  518.8 143.8 %all-gather.16.cloned.1.call-start = ((), (), s32[]{:S(2)}) async-start(), calls=%async_computation.10 | async-start | bytes 8355840 | tf_op jit(solution)/shard_map/all_gather | solution.py:208
  662.6 8.9 %copy-start.30 = (f32[1280]{0:T(1024)S(1)}, f32[1280]{0:T(1024)}, u32[]{:S(2)}) copy-start(f32[1280]{0:T(1024)} %param.41) | copy-start | bytes 15364
  (24 other events, 64.8 us)
Sparse Core Ops, SparseCore 0:
  10.9 25.1 all-reduce.23
  37.7 27.1 all-gather.9
  71.1 25.6 all-gather.11
  98.8 59.2 all-gather.7
  162.4 9.8 reduce-scatter.3
  227.7 57.3 reduce-scatter.5
  288.6 55.5 reduce-scatter.7
  346.8 19.9 all-reduce.19
  370.6 93.8 all-reduce.17
  478.1 38.1 all-reduce.21
  518.9 71.5 all-gather.13
  592.7 69.9 all-gather.15
